TPU v7x, 512 devices: a whole 4x4x16 slice. The times are simulated.
512 devices in a mesh: wide: 128 (over y, z, core), narrow: 4 (over x).
Axes of the slice: x: 4, y: 4, z: 16, core: 2. Of those that a mesh axis runs over, the one named last changes fastest.
Arguments:
- raw_echo: bfloat16 [2, 4, 1024, 16384], P(None, 'narrow', 'wide'), may hold values from -6 to 6
- range_replica: bfloat16 [2, 4096], replicated, may hold values from -0.0625 to 0.0625
- interp_weight: float32 [8, 1024], replicated, may hold values from -2.5 to 2.5
- band_offset: int32 [16384], P('wide'), may hold values from 0 to 24, as said below
- azimuth_rate: float32 [16384], P('wide'), may hold values from 0.01 to 0.1
- tile_owner: int32 [4, 16], replicated, may hold values from 0 to 3, as said below
Outputs:
- tile_mean: float32 [4, 64, 16384], P('narrow', None, 'wide')
Inputs may be any that keep to these rules, and one draw needn't show every extreme that they name: band_offset reaches 24 in every draw. `tile_owner`: every tile owns at least one block of every group. One tile, the same for every group, owns exactly 8 blocks of every group; no tile owns more than 8 blocks of one group.
All inputs are finite; a program needn't handle non-finite values.
Results may differ from a plain program's by a relative error of at most 0.011.
Values may be sent and summed in bfloat16 or wider, within the bound.
No kernel may reach another device: no remote copies, remote signals or barrier semaphores. Data moves between devices by JAX's collectives and lax.ppermute only.
A program may use at most 64 MiB of HBM per device.

v0:
```python
import math
import jax
import jax.numpy as jnp
from jax import lax
from jax.sharding import PartitionSpec as P

RSPLIT = 128
PUL_DEV = 8
CAP = 8
HALO = 31


def passed_along(shard, axis, by):
    devices = lax.axis_size(axis)
    pairs = [(i, i + by) for i in range(devices) if 0 <= i + by < devices]
    return lax.ppermute(shard, axis, pairs)


def make_table(size, sign):
    index = jnp.arange(size, dtype=jnp.int32)
    product = index[:, None] * index[None, :] % size
    angle = sign * 2.0 * math.pi / size * product.astype(jnp.float32)
    norm = 1.0 / math.sqrt(size)
    return (
        (jnp.cos(angle) * norm).astype(jnp.bfloat16),
        (jnp.sin(angle) * norm).astype(jnp.bfloat16),
    )


def make_twiddle(first, second, sign):
    heads = jnp.arange(first, dtype=jnp.int32)
    tails = jnp.arange(second, dtype=jnp.int32)
    product = heads[:, None] * tails[None, :] % (first * second)
    angle = sign * 2.0 * math.pi / (first * second) * product.astype(jnp.float32)
    return (jnp.cos(angle), jnp.sin(angle))


def range_transform(real_part, imag_part, first, sign):
    count = real_part.shape[0]
    length = real_part.shape[1]
    second = length // first
    head_cos, head_sin = make_table(first, sign)
    tail_cos, tail_sin = make_table(second, sign)
    twist_cos, twist_sin = make_twiddle(first, second, sign)
    split_real = real_part.reshape(count, first, second)
    split_imag = imag_part.reshape(count, first, second)

    def section_one(table, values):
        return jnp.einsum("kn,pnm->pkm", table, values, preferred_element_type=jnp.float32)

    mid_real = section_one(head_cos, split_real) - section_one(head_sin, split_imag)
    mid_imag = section_one(head_cos, split_imag) + section_one(head_sin, split_real)
    turn_real = (mid_real * twist_cos - mid_imag * twist_sin).astype(jnp.bfloat16)
    turn_imag = (mid_real * twist_sin + mid_imag * twist_cos).astype(jnp.bfloat16)

    def section_two(table, values):
        return jnp.einsum("pam,km->pka", values, table, preferred_element_type=jnp.float32)

    out_real = section_two(tail_cos, turn_real) - section_two(tail_sin, turn_imag)
    out_imag = section_two(tail_cos, turn_imag) + section_two(tail_sin, turn_real)
    return (out_real.reshape(count, length), out_imag.reshape(count, length))


def pulse_transform(real_part, imag_part, first, sign):
    length = real_part.shape[0]
    width = real_part.shape[1]
    second = length // first
    head_cos, head_sin = make_table(first, sign)
    tail_cos, tail_sin = make_table(second, sign)
    twist_cos, twist_sin = make_twiddle(first, second, sign)
    twist_cos = twist_cos[:, :, None]
    twist_sin = twist_sin[:, :, None]
    split_real = real_part.reshape(first, second, width)
    split_imag = imag_part.reshape(first, second, width)

    def section_one(table, values):
        return jnp.einsum("kn,nmc->kmc", table, values, preferred_element_type=jnp.float32)

    mid_real = section_one(head_cos, split_real) - section_one(head_sin, split_imag)
    mid_imag = section_one(head_cos, split_imag) + section_one(head_sin, split_real)
    turn_real = (mid_real * twist_cos - mid_imag * twist_sin).astype(jnp.bfloat16)
    turn_imag = (mid_real * twist_sin + mid_imag * twist_cos).astype(jnp.bfloat16)

    def section_two(table, values):
        return jnp.einsum("kmc,jm->jkc", values, table, preferred_element_type=jnp.float32)

    out_real = section_two(tail_cos, turn_real) - section_two(tail_sin, turn_imag)
    out_imag = section_two(tail_cos, turn_imag) + section_two(tail_sin, turn_real)
    return (out_real.reshape(length, width), out_imag.reshape(length, width))


def azimuth_spectra(values):
    first_real, first_imag = pulse_transform(values[0, :, 0], values[1, :, 0], PUL_DEV, -1)
    return jnp.stack([first_real.astype(jnp.bfloat16), first_imag.astype(jnp.bfloat16)])[
        :, :, None, :
    ]


def per_device(raw_echo, range_replica, interp_weight, band_offset, azimuth_rate, tile_owner):
    echo = raw_echo[:, 0]
    length = echo.shape[2]
    padded = jnp.pad(range_replica, ((0, 0), (0, length - range_replica.shape[1])))
    replica_real, replica_imag = range_transform(padded[0:1], padded[1:2], RSPLIT, -1)
    scale = math.sqrt(length)
    replica_real = replica_real[0] * scale
    replica_imag = replica_imag[0] * scale
    spec_real, spec_imag = range_transform(echo[0], echo[1], RSPLIT, -1)
    match_real = (spec_real * replica_real + spec_imag * replica_imag).astype(jnp.bfloat16)
    match_imag = (spec_imag * replica_real - spec_real * replica_imag).astype(jnp.bfloat16)
    comp_real, comp_imag = range_transform(match_real, match_imag, RSPLIT, 1)
    compressed = jnp.stack([comp_real.astype(jnp.bfloat16), comp_imag.astype(jnp.bfloat16)])
    devices = lax.axis_size("wide")
    width = length // devices
    local_pulses = compressed.shape[1]
    split_bins = compressed.reshape(2, local_pulses, devices, width)
    doppler = azimuth_spectra(
        lax.all_to_all(split_bins, "wide", split_axis=2, concat_axis=1, tiled=True)
    )[:, :, 0]
    rim = passed_along(doppler[:, :, :HALO], "wide", -1)
    extended = jnp.concatenate([doppler, rim], axis=2)
    pulses = extended.shape[1]
    columns = jnp.arange(width + HALO, dtype=jnp.int32)
    bins = jnp.arange(width, dtype=jnp.int32) + band_offset
    moved_real = jnp.zeros((pulses, width), jnp.float32)
    moved_imag = jnp.zeros((pulses, width), jnp.float32)
    for tap_index in range(interp_weight.shape[0]):
        select = (columns[:, None] == (bins + tap_index)[None, :]).astype(jnp.bfloat16)
        picked = jnp.einsum("xpc,cr->xpr", extended, select, preferred_element_type=jnp.float32)
        weight = interp_weight[tap_index][:, None]
        moved_real = moved_real + weight * picked[0]
        moved_imag = moved_imag + weight * picked[1]
    freq = jnp.arange(pulses, dtype=jnp.int32)
    shifted = ((freq + pulses // 2) % pulses - pulses // 2).astype(jnp.float32) / pulses
    phase = math.pi * (shifted * shifted)[:, None] / azimuth_rate[None, :]
    phase_cos = jnp.cos(phase)
    phase_sin = jnp.sin(phase)
    focus_real = (moved_real * phase_cos - moved_imag * phase_sin).astype(jnp.bfloat16)
    focus_imag = (moved_real * phase_sin + moved_imag * phase_cos).astype(jnp.bfloat16)
    image_real, image_imag = pulse_transform(focus_real, focus_imag, PUL_DEV, 1)
    intensity = (image_real * image_real + image_imag * image_imag).astype(jnp.bfloat16)
    block_count = tile_owner.shape[1]
    block_rows = pulses // block_count
    blocks = intensity.reshape(block_count, block_rows, width)
    tiles = lax.axis_size("narrow")
    group = lax.axis_index("narrow")
    tile_ids = jnp.arange(tiles, dtype=jnp.int32)
    own_row = lax.dynamic_slice_in_dim(tile_owner, group, 1, 0)[0]
    member = (own_row[None, :] == tile_ids[:, None]).astype(jnp.int32)
    counts = jnp.sum(
        (tile_owner[:, :, None] == tile_ids[None, None, :]).astype(jnp.int32), axis=(0, 1)
    )
    own_count = jnp.sum(jnp.where(tile_ids == group, counts, 0)).astype(jnp.float32)
    rank = jnp.cumsum(member, axis=1) - 1
    slots = jnp.arange(CAP, dtype=jnp.int32)
    select_slots = ((member[:, None, :] == 1) & (rank[:, None, :] == slots[None, :, None])).astype(
        jnp.bfloat16
    )
    outgoing = jnp.einsum(
        "tsb,bir->tsir", select_slots, blocks, preferred_element_type=jnp.float32
    ).astype(jnp.bfloat16)
    incoming = lax.all_to_all(outgoing, "narrow", split_axis=0, concat_axis=0, tiled=True)
    summed = jnp.sum(incoming, axis=(0, 1), dtype=jnp.float32)[None]
    return summed / own_count


def solution(mesh):
    return jax.shard_map(
        per_device,
        mesh=mesh,
        in_specs=(P(None, "narrow", "wide", None), P(), P(), P("wide"), P("wide"), P()),
        out_specs=P("narrow", None, "wide"),
        check_vma=False,
    )
```

profile of v0, /device:TPU:9, one launch (start us, length us, event | category | flops | bytes accessed | tf_op | source)
XLA Modules:
  0.0 111.7 jit_solution(6334069500444813462)
XLA Ops:
  0.8 1.1 slice_bitcast_fusion.1
  3.2 0.5 fusion.31
  6.4 0.6 fusion.112
  8.5 0.5 fusion.32
  10.6 0.6 subtract_convert_fusion.3
  13.0 1.1 %copy.222 = bf16[2,8,128,128]{3,1,0,2:T(8,128)(2,1)} copy(bf16[2,8,128,128]{3,2,1,0:T(8,128)(2,1)S(1)} %pad_maximum_fusion.1) | data formatting | bytes 1048576 | tf_op jit(solution)/shard_map/stack | solution.py:111
  14.1 20.1 %all-to-all-start = ((bf16[2,8,128,128]{3,1,0,2:T(8,128)(2,1)}), bf16[2,8,128,128]{3,1,0,2:T(8,128)(2,1)S(1)}, u32[]{:S(2)}, u32[]{:S(2)}) async-start(bf16[2,8,128,128]{3,1,0,2:T(8,128)(2,1)} %copy.222), calls=%async_computation | async-start | bytes 1048576 | tf_op jit(solution)/shard_map/all_to_all | solution.py:117
  36.1 30.7 %all-to-all-done = bf16[2,8,128,128]{3,1,0,2:T(8,128)(2,1)S(1)} async-done(((bf16[2,8,128,128]{3,1,0,2:T(8,128)(2,1)}), bf16[2,8,128,128]{3,1,0,2:T(8,128)(2,1)S(1)}, u32[]{:S(2)}, u32[]{:S(2)}) %all-to-all-start) | async-done | bytes 524320 | tf_op jit(solution)/shard_map/all_to_all | solution.py:117
  70.8 3.3 %collective-permute-start = (bf16[2,1024,31]{1,2,0:T(8,128)(2,1)S(1)}, bf16[2,1024,31]{1,2,0:T(8,128)(2,1)S(1)}, u32[]{:S(2)}, u32[]{:S(2)}) collective-permute-start(bf16[2,1024,31]{1,2,0:T(8,128)(2,1)S(1)} %pad_maximum_fusion.2), channel_id=1, source_target_pairs={{4,0},{8,4},{12,8},{16,12},{20,16},{24,20},{28,24},{32,28},{36,32}... | collective-permute-start | bytes 380936 | tf_op jit(solution)/shard_map/ppermute | solution.py:16
  74.1 3.3 %collective-permute-done = bf16[2,1024,31]{1,2,0:T(8,128)(2,1)S(1)} collective-permute-done((bf16[2,1024,31]{1,2,0:T(8,128)(2,1)S(1)}, bf16[2,1024,31]{1,2,0:T(8,128)(2,1)S(1)}, u32[]{:S(2)}, u32[]{:S(2)}) %collective-permute-start) | collective-permute-done | bytes 127008 | tf_op jit(solution)/shard_map/ppermute | solution.py:16
  77.9 0.5 fusion.68
  78.5 0.5 fusion.71
  79.0 0.5 fusion.74
  80.2 0.5 fusion.80
  80.7 0.5 fusion.83
  81.3 0.5 fusion.86
  81.9 0.6 copy-done.2
  82.5 7.7 %subtract_convert_fusion.1 = (bf16[8,128,128]{2,0,1:T(8,128)(2,1)S(1)}, f32[8,128,128]{2,0,1:T(8,128)S(1)}, f32[8,128,128]{2,0,1:T(8,128)S(1)}) fusion(f32[128]{0:T(128)S(1)} %copy-done.2, f32[8,128]{0,1:T(8,128)S(1)} %copy.253, f32[8,128,128]{2,1,0:T(8,128)S(1)} %bitcast.245, f32[8,128]{0,1:T(8,128)S(1)} %copy.251, f32[8,128,128]{2,1,0:T(8,128)S(1)} %bitcast.243, ...), kind=kLoop, calls=%fused_computation.74 | loop fusion | flops 4587520 | bytes 9736704 | tf_op jit(solution)/shard_map/convert_element_type | solution.py:137
  90.4 2.5 %add_convert_fusion.1 = bf16[8,128,128]{2,0,1:T(8,128)(2,1)S(1)} fusion(f32[8,128,128]{2,0,1:T(8,128)S(1)} %get-tuple-element.9, f32[8,128,128]{2,0,1:T(8,128)S(1)} %get-tuple-element.8, f32[128]{0:T(128)S(1)} %copy-done.2, f32[8,128]{0,1:T(8,128)S(1)} %copy.253), kind=kLoop, calls=%fused_computation.73 | loop fusion | flops 655360 | bytes 1315328 | tf_op jit(solution)/shard_map/convert_element_type | solution.py:138
  95.9 1.1 convolution_convert_fusion
  97.0 4.0 %all-to-all-start.1 = ((bf16[4,8,64,128]{3,1,2,0:T(8,128)(2,1)}), bf16[4,8,64,128]{3,1,2,0:T(8,128)(2,1)S(1)}, u32[]{:S(2)}, u32[]{:S(2)}) async-start(bf16[4,8,64,128]{3,1,2,0:T(8,128)(2,1)} %convolution_convert_fusion), calls=%async_computation.1 | async-start | bytes 1048576 | tf_op jit(solution)/shard_map/all_to_all | solution.py:161
  101.1 0.6 fusion.191
  102.4 8.6 %all-to-all-done.1 = bf16[4,8,64,128]{3,1,2,0:T(8,128)(2,1)S(1)} async-done(((bf16[4,8,64,128]{3,1,2,0:T(8,128)(2,1)}), bf16[4,8,64,128]{3,1,2,0:T(8,128)(2,1)S(1)}, u32[]{:S(2)}, u32[]{:S(2)}) %all-to-all-start.1) | async-done | bytes 524320 | tf_op jit(solution)/shard_map/all_to_all | solution.py:161
  111.1 0.6 divide_bitcast_fusion
  (96 shorter events, 20.2 us)
Async XLA Ops:
  4.2 0.9 copy-start.1
  13.0 21.5 %copy-start = (f32[8,1024]{1,0:T(8,128)S(1)}, f32[8,1024]{1,0:T(8,128)}, u32[]{:S(2)}) copy-start(f32[8,1024]{1,0:T(8,128)} %param.8) | copy-start | bytes 98308
  14.1 21.7 %copy-start.3 = (s32[4,16]{1,0:T(4,128)S(1)}, s32[4,16]{1,0:T(4,128)}, u32[]{:S(2)}) copy-start(s32[4,16]{1,0:T(4,128)} %param.11) | copy-start | bytes 772
  14.1 21.9 %copy-start.4 = (s32[128]{0:T(128)S(1)}, s32[128]{0:T(128)}, u32[]{:S(2)}) copy-start(s32[128]{0:T(128)} %param.9) | copy-start | bytes 1540
  14.1 52.7 %all-to-all-start = ((bf16[2,8,128,128]{3,1,0,2:T(8,128)(2,1)}), bf16[2,8,128,128]{3,1,0,2:T(8,128)(2,1)S(1)}, u32[]{:S(2)}, u32[]{:S(2)}) async-start(bf16[2,8,128,128]{3,1,0,2:T(8,128)(2,1)} %copy.222), calls=%async_computation | async-start | bytes 1048576 | tf_op jit(solution)/shard_map/all_to_all | solution.py:117
  70.8 6.6 %collective-permute-start = (bf16[2,1024,31]{1,2,0:T(8,128)(2,1)S(1)}, bf16[2,1024,31]{1,2,0:T(8,128)(2,1)S(1)}, u32[]{:S(2)}, u32[]{:S(2)}) collective-permute-start(bf16[2,1024,31]{1,2,0:T(8,128)(2,1)S(1)} %pad_maximum_fusion.2), channel_id=1, source_target_pairs={{4,0},{8,4},{12,8},{16,12},{20,16},{24,20},{28,24},{32,28},{36,32}... | collective-permute-start | bytes 380936 | tf_op jit(solution)/shard_map/ppermute | solution.py:16
  81.8 0.7 copy-start.2
  97.0 14.0 %all-to-all-start.1 = ((bf16[4,8,64,128]{3,1,2,0:T(8,128)(2,1)}), bf16[4,8,64,128]{3,1,2,0:T(8,128)(2,1)S(1)}, u32[]{:S(2)}, u32[]{:S(2)}) async-start(bf16[4,8,64,128]{3,1,2,0:T(8,128)(2,1)} %convolution_convert_fusion), calls=%async_computation.1 | async-start | bytes 1048576 | tf_op jit(solution)/shard_map/all_to_all | solution.py:161
where the time goes:
time: 112 us
  waiting for transfers between devices  42.6 us (38%)
  starting transfers between devices  27.4 us (24%)
  matrix products  21.6 us (19%)
  other arithmetic  13 us (12%)
  local copies, waits for them, and re-layouts  5.95 us (5%)
  between operations  1.22 us (1%)
    all_to_all x1, waiting for transfers between devices, per_device(): lax.all_to_all(split_bins, 'wide', split_axis=2, concat_axis=1, tiled=True)  30.7 us
    all_to_all x1, starting transfers between devices, per_device(): lax.all_to_all(split_bins, 'wide', split_axis=2, concat_axis=1, tiled=True)  20.1 us
    all_to_all x1, waiting for transfers between devices, per_device(): lax.all_to_all(outgoing, 'narrow', split_axis=0, concat_axis=0, tiled=True)  8.59 us
    convert_element_type x1, other arithmetic, per_device(): (moved_real * phase_cos - moved_imag * phase_sin).astype(jnp.bfloat16)  7.7 us
    dot_general x12, matrix products, section_one(): jnp.einsum('kn,pnm->pkm', table, values, preferred_element_type=jnp.float32)  5.54 us
    dot_general x12, matrix products, section_two(): jnp.einsum('pam,km->pka', values, table, preferred_element_type=jnp.float32)  5.01 us
    all_to_all x1, starting transfers between devices, per_device(): lax.all_to_all(outgoing, 'narrow', split_axis=0, concat_axis=0, tiled=True)  3.99 us
    dot_general x8, matrix products, per_device(): jnp.einsum('xpc,cr->xpr', extended, select, preferred_element_type=jnp.fl...  3.83 us
  transfers between devices with their start and end apart: 3, of which 3 were waited for; matrix products, arithmetic and copies ran while one was open for 2% of the time, Pallas kernels for 0%

commit v1 on v0

--- a/solution.py
+++ b/solution.py
@@ -8,6 +8,16 @@
 PUL_DEV = 8
 CAP = 8
 HALO = 31
+
+
+def _expand_regions(piece_in, peer_axis):
+    inter = jnp.concatenate(
+        lax.all_to_all(
+            jnp.stack(jnp.split(piece_in, lax.axis_size(peer_axis), 2)), peer_axis, 0, 0
+        ),
+        1,
+    )
+    return inter
 
 
 def passed_along(shard, axis, by):
@@ -113,9 +123,7 @@
     width = length // devices
     local_pulses = compressed.shape[1]
     split_bins = compressed.reshape(2, local_pulses, devices, width)
-    doppler = azimuth_spectra(
-        lax.all_to_all(split_bins, "wide", split_axis=2, concat_axis=1, tiled=True)
-    )[:, :, 0]
+    doppler = azimuth_spectra(_expand_regions(split_bins, "wide"))[:, :, 0]
     rim = passed_along(doppler[:, :, :HALO], "wide", -1)
     extended = jnp.concatenate([doppler, rim], axis=2)
     pulses = extended.shape[1]

time: 112 us -> 183 us (1.63)
  local copies, waits for them, and re-layouts: 5.95 us -> 79.5 us
  other arithmetic: 13 us -> 9.6 us
    unnamed x11 -> x138, local copies, waits for them, and re-layouts: 1.66 us -> 76.7 us
    convert_element_type x1, other arithmetic: 7.7 us -> 3.15 us  [per_device(): (moved_real * phase_cos - moved_imag * phase_sin).astype(jnp.bfloat16)]
  transfers between devices with their start and end apart: 3 -> 3, of which waited for: 3 -> 3; matrix products, arithmetic and copies ran while one was open for 2% -> 1% of each run, Pallas kernels for 0% -> 0%
where the time goes in v1:
time: 183 us
  local copies, waits for them, and re-layouts  79.5 us (43%)
  waiting for transfers between devices  43.5 us (24%)
  starting transfers between devices  27.2 us (15%)
  matrix products  21.8 us (12%)
  other arithmetic  9.6 us (5%)
    unnamed x138, local copies, waits for them, and re-layouts  76.7 us
    all_to_all x1, waiting for transfers between devices, _expand_regions(): lax.all_to_all(jnp.stack(jnp.split(piece_in, lax.axis_size(peer_axis), 2)...  31.9 us
    all_to_all x1, starting transfers between devices, _expand_regions(): lax.all_to_all(jnp.stack(jnp.split(piece_in, lax.axis_size(peer_axis), 2)...  19.9 us
    all_to_all x1, waiting for transfers between devices, per_device(): lax.all_to_all(outgoing, 'narrow', split_axis=0, concat_axis=0, tiled=True)  8.59 us
    dot_general x12, matrix products, section_one(): jnp.einsum('kn,pnm->pkm', table, values, preferred_element_type=jnp.float32)  5.54 us
    dot_general x12, matrix products, section_two(): jnp.einsum('pam,km->pka', values, table, preferred_element_type=jnp.float32)  5.01 us
    all_to_all x1, starting transfers between devices, per_device(): lax.all_to_all(outgoing, 'narrow', split_axis=0, concat_axis=0, tiled=True)  3.99 us
    dot_general x8, matrix products, per_device(): jnp.einsum('xpc,cr->xpr', extended, select, preferred_element_type=jnp.fl...  3.84 us
  transfers between devices with their start and end apart: 3, of which 3 were waited for; matrix products, arithmetic and copies ran while one was open for 1% of the time, Pallas kernels for 0%

profile of v1, /device:TPU:9, one launch (start us, length us, event | category | flops | bytes accessed | tf_op | source)
XLA Modules:
  0.0 183.0 jit_solution(7247206582401609212)
XLA Ops:
  0.8 1.1 slice_bitcast_fusion.1
  23.3 0.6 constant_dynamic-update-slice_fusion.112
  28.1 0.6 constant_dynamic-update-slice_fusion.104
  45.2 0.6 constant_dynamic-update-slice_fusion.75
  45.8 0.6 constant_dynamic-update-slice_fusion.74
  49.9 0.6 constant_dynamic-update-slice_fusion.67
  55.3 0.6 constant_dynamic-update-slice_fusion.58
  58.2 0.6 constant_dynamic-update-slice_fusion.53
  68.2 0.6 constant_dynamic-update-slice_fusion.36
  72.4 0.6 constant_dynamic-update-slice_fusion.29
  80.1 0.6 constant_dynamic-update-slice_fusion.16
  84.2 0.6 constant_dynamic-update-slice_fusion.9
  89.6 0.6 constant_dynamic-update-slice_fusion
  90.2 19.9 %all-to-all-start = ((bf16[128,2,8,1,128]{4,2,1,3,0:T(8,128)(2,1)}), bf16[128,2,8,1,128]{4,2,1,3,0:T(8,128)(2,1)S(1)}, u32[]{:S(2)}, u32[]{:S(2)}) async-start(bf16[128,2,8,1,128]{4,2,1,3,0:T(8,128)(2,1)} %constant_dynamic-update-slice_fusion), calls=%async_computation | async-start | bytes 1048576 | tf_op jit(solution)/shard_map/all_to_all | solution.py:15
  110.8 31.9 %all-to-all-done = bf16[128,2,8,1,128]{4,2,1,3,0:T(8,128)(2,1)S(1)} async-done(((bf16[128,2,8,1,128]{4,2,1,3,0:T(8,128)(2,1)}), bf16[128,2,8,1,128]{4,2,1,3,0:T(8,128)(2,1)S(1)}, u32[]{:S(2)}, u32[]{:S(2)}) %all-to-all-start) | async-done | bytes 524320 | tf_op jit(solution)/shard_map/all_to_all | solution.py:15
  146.6 3.3 %collective-permute-start = (bf16[2,1024,31]{1,2,0:T(8,128)(2,1)S(1)}, bf16[2,1024,31]{1,2,0:T(8,128)(2,1)S(1)}, u32[]{:S(2)}, u32[]{:S(2)}) collective-permute-start(bf16[2,1024,31]{1,2,0:T(8,128)(2,1)S(1)} %pad_maximum_fusion.1), channel_id=1, source_target_pairs={{4,0},{8,4},{12,8},{16,12},{20,16},{24,20},{28,24},{32,28},{36,32}... | collective-permute-start | bytes 380936 | tf_op jit(solution)/shard_map/ppermute | solution.py:26
  150.2 3.0 %collective-permute-done = bf16[2,1024,31]{1,2,0:T(8,128)(2,1)S(1)} collective-permute-done((bf16[2,1024,31]{1,2,0:T(8,128)(2,1)S(1)}, bf16[2,1024,31]{1,2,0:T(8,128)(2,1)S(1)}, u32[]{:S(2)}, u32[]{:S(2)}) %collective-permute-start) | collective-permute-done | bytes 127008 | tf_op jit(solution)/shard_map/ppermute | solution.py:26
  158.3 3.2 %subtract_convert_fusion.1 = (bf16[8,128,128]{2,1,0:T(8,128)(2,1)S(1)}, f32[8,128,128]{2,1,0:T(8,128)S(1)}, f32[8,128,128]{2,1,0:T(8,128)S(1)}) fusion(f32[128]{0:T(128)S(1)} %copy-done.2, f32[8,128]{1,0:T(8,128)S(1)} %fusion.288, f32[8,128,128]{2,1,0:T(8,128)S(1)} %bitcast.494, f32[8,128]{1,0:T(8,128)S(1)} %bitcast.506, f32[8,128,128]{2,1,0:T(8,128)S(1)} %bitcast.492, ...), kind=kLoop, calls=%fused_computation.296 | loop fusion | flops 4587520 | bytes 9736704 | tf_op jit(solution)/shard_map/convert_element_type | solution.py:145
  161.8 2.3 %add_convert_fusion.1 = bf16[8,128,128]{2,1,0:T(8,128)(2,1)S(1)} fusion(f32[8,128,128]{2,1,0:T(8,128)S(1)} %get-tuple-element.9, f32[8,128,128]{2,1,0:T(8,128)S(1)} %get-tuple-element.8, f32[128]{0:T(128)S(1)} %copy-done.2, f32[8,128]{1,0:T(8,128)S(1)} %fusion.288), kind=kLoop, calls=%fused_computation.295 | loop fusion | flops 655360 | bytes 1315328 | tf_op jit(solution)/shard_map/convert_element_type | solution.py:146
  167.1 1.1 convolution_convert_fusion
  168.2 4.0 %all-to-all-start.1 = ((bf16[4,8,64,128]{3,1,2,0:T(8,128)(2,1)}), bf16[4,8,64,128]{3,1,2,0:T(8,128)(2,1)S(1)}, u32[]{:S(2)}, u32[]{:S(2)}) async-start(bf16[4,8,64,128]{3,1,2,0:T(8,128)(2,1)} %convolution_convert_fusion), calls=%async_computation.1 | async-start | bytes 1048576 | tf_op jit(solution)/shard_map/all_to_all | solution.py:169
  172.3 0.6 fusion.308
  173.6 8.6 %all-to-all-done.1 = bf16[4,8,64,128]{3,1,2,0:T(8,128)(2,1)S(1)} async-done(((bf16[4,8,64,128]{3,1,2,0:T(8,128)(2,1)}), bf16[4,8,64,128]{3,1,2,0:T(8,128)(2,1)S(1)}, u32[]{:S(2)}, u32[]{:S(2)}) %all-to-all-start.1) | async-done | bytes 524320 | tf_op jit(solution)/shard_map/all_to_all | solution.py:169
  182.4 0.6 divide_bitcast_fusion
  (227 shorter events, 94.8 us)
Async XLA Ops:
  4.2 0.9 copy-start.1
  52.9 57.5 %copy-start.3 = (s32[4,16]{1,0:T(4,128)S(1)}, s32[4,16]{1,0:T(4,128)}, u32[]{:S(2)}) copy-start(s32[4,16]{1,0:T(4,128)} %param.11) | copy-start | bytes 772
  54.1 56.7 %copy-start.4 = (s32[128]{0:T(128)S(1)}, s32[128]{0:T(128)}, u32[]{:S(2)}) copy-start(s32[128]{0:T(128)} %param.9) | copy-start | bytes 1540
  54.1 56.7 %copy-start = (f32[8,1024]{1,0:T(8,128)S(1)}, f32[8,1024]{1,0:T(8,128)}, u32[]{:S(2)}) copy-start(f32[8,1024]{1,0:T(8,128)} %param.8) | copy-start | bytes 98308
  90.2 52.5 %all-to-all-start = ((bf16[128,2,8,1,128]{4,2,1,3,0:T(8,128)(2,1)}), bf16[128,2,8,1,128]{4,2,1,3,0:T(8,128)(2,1)S(1)}, u32[]{:S(2)}, u32[]{:S(2)}) async-start(bf16[128,2,8,1,128]{4,2,1,3,0:T(8,128)(2,1)} %constant_dynamic-update-slice_fusion), calls=%async_computation | async-start | bytes 1048576 | tf_op jit(solution)/shard_map/all_to_all | solution.py:15
  146.6 6.6 %collective-permute-start = (bf16[2,1024,31]{1,2,0:T(8,128)(2,1)S(1)}, bf16[2,1024,31]{1,2,0:T(8,128)(2,1)S(1)}, u32[]{:S(2)}, u32[]{:S(2)}) collective-permute-start(bf16[2,1024,31]{1,2,0:T(8,128)(2,1)S(1)} %pad_maximum_fusion.1), channel_id=1, source_target_pairs={{4,0},{8,4},{12,8},{16,12},{20,16},{24,20},{28,24},{32,28},{36,32}... | collective-permute-start | bytes 380936 | tf_op jit(solution)/shard_map/ppermute | solution.py:26
  157.7 0.7 copy-start.2
  168.2 14.0 %all-to-all-start.1 = ((bf16[4,8,64,128]{3,1,2,0:T(8,128)(2,1)}), bf16[4,8,64,128]{3,1,2,0:T(8,128)(2,1)S(1)}, u32[]{:S(2)}, u32[]{:S(2)}) async-start(bf16[4,8,64,128]{3,1,2,0:T(8,128)(2,1)} %convolution_convert_fusion), calls=%async_computation.1 | async-start | bytes 1048576 | tf_op jit(solution)/shard_map/all_to_all | solution.py:169
